TPU v7x, 256 devices: a whole 4x4x8 slice. The times are simulated.
256 devices in a mesh: col: 32 (over z, x), row: 8 (over y, core).
Axes of the slice: x: 4, y: 4, z: 8, core: 2. Of those that a mesh axis runs over, the one named last changes fastest.
Arguments:
- right_side: float32 [6, 64, 64, 128], P(None, 'row'), may hold values from -6 to 6
- lower_blocks: bfloat16 [15, 64, 64, 128, 128], P(None, 'row', 'col'), may hold values from -0.078125 to 0.078125
- pattern: int32 [15, 64, 64], P(None, 'row', 'col'), may hold values 0 or 1
- diag_inverse: bfloat16 [6, 64, 128, 128], P(None, 'row'), may hold values from -2 to 2
Outputs:
- solution: float32 [6, 64, 64, 128], P(None, 'col')
All inputs are finite; a program needn't handle non-finite values. No bound on the sum of `pattern` on one device may be relied on, other than what follows from the above.
Results may differ from a plain program's by a relative error of at most 0.0029.
Values sent between devices are 32-bit elements; how exact they have to be, the bound alone decides.
No kernel may reach another device: no remote copies, remote signals or barrier semaphores. Data moves between devices by JAX's collectives and lax.ppermute only.
A program may use at most 64 MiB of HBM per device.

v0:
```python
import jax
import jax.numpy as jnp
from jax import lax
from jax.sharding import PartitionSpec as P


def broadcast(shard, axis, root):
    mine = lax.axis_index(axis) == root
    return lax.psum(jnp.where(mine, shard, jnp.zeros_like(shard)), axis)


def solve_rows(residual, inverse):
    return jnp.einsum(
        "pnb,pbd->pnd", residual, inverse.astype(jnp.float32), precision=lax.Precision.HIGHEST
    )


def body(right_side, lower_blocks, pattern, diag_inverse):
    row_count = right_side.shape[1]
    col_count = pattern.shape[2]
    col_id = lax.axis_index("col")
    source = col_id * col_count // row_count
    first_row = col_id * col_count - source * row_count
    solved = []
    outputs = []
    for section in range(right_side.shape[0]):
        rhs_section = right_side[section]
        inv_section = diag_inverse[section]
        if section > 0:
            offset = section * (section - 1) // 2
            blocks = lower_blocks[offset : offset + section]
            weights = pattern[offset : offset + section].astype(jnp.float32)
            earlier = jnp.stack(solved)
            products = jnp.einsum(
                "lcnb,lrcbd->lrcnd", earlier, blocks, preferred_element_type=jnp.float32
            )
            partial_value = jnp.sum(weights[:, :, :, None, None] * products, axis=(0, 2))
            totals = lax.psum(partial_value, "col")
            row_solved = solve_rows(rhs_section - totals, inv_section)
            owned = lax.dynamic_slice_in_dim(row_solved, first_row, col_count, 0)
        else:
            owned_rhs = lax.dynamic_slice_in_dim(rhs_section, first_row, col_count, 0)
            owned_inv = lax.dynamic_slice_in_dim(inv_section, first_row, col_count, 0)
            owned = solve_rows(owned_rhs, owned_inv)
        segment = broadcast(owned, "row", source)
        outputs.append(segment)
        solved.append(segment.astype(jnp.bfloat16))
    return jnp.stack(outputs)


def solution(mesh):
    placed = (
        P(None, "row", None, None),
        P(None, "row", "col", None, None),
        P(None, "row", "col"),
        P(None, "row", None, None),
    )
    return jax.shard_map(
        body, mesh=mesh, in_specs=placed, out_specs=P(None, "col", None, None), check_vma=False
    )
```

profile of v0, /device:TPU:2, one launch (start us, length us, event | category | flops | bytes accessed | tf_op | source)
XLA Modules:
  0.0 1147.2 jit_solution(12751743245303424274)
XLA Ops:
  6.5 1.1 slice.66
  7.6 1.0 slice.67
  8.6 0.8 convolution_select_fusion
  9.5 0.8 copy.32
  10.3 67.2 %all-reduce.12.cloned.1.call-done = f32[2,64,128]{2,1,0:T(8,128)} async-done(((f32[2,64,128]{2,1,0:T(8,128)}), f32[2,64,128]{2,1,0:T(8,128)}) %all-reduce.12.cloned.1.call-update) | async-done | bytes 65552 | tf_op jit(solution)/shard_map/psum | solution.py:9
  77.6 2.1 fusion.12
  79.8 0.1 copy.34
  79.9 0.1 copy.20
  80.0 144.3 %all-reduce.14.cloned.1.call-done = f32[8,64,128]{2,1,0:T(8,128)} async-done(((f32[8,64,128]{2,1,0:T(8,128)}), f32[8,64,128]{2,1,0:T(8,128)}) %all-reduce.14.cloned.1.call-update) | async-done | bytes 262160 | tf_op jit(solution)/shard_map/psum | solution.py:38
  224.3 1.4 fusion.28
  225.6 0.6 dynamic-slice_select_fusion.3
  226.4 63.3 %all-reduce.16.cloned.1.call-done = f32[2,64,128]{2,1,0:T(8,128)} async-done(((f32[2,64,128]{2,1,0:T(8,128)}), f32[2,64,128]{2,1,0:T(8,128)}) %all-reduce.16.cloned.1.call-update) | async-done | bytes 65552 | tf_op jit(solution)/shard_map/psum | solution.py:9
  289.7 0.9 constant_dynamic-update-slice_fusion.2
  290.6 2.2 fusion.10
  292.9 143.4 %all-reduce.18.cloned.1.call-done = f32[8,64,128]{2,1,0:T(8,128)} async-done(((f32[8,64,128]{2,1,0:T(8,128)}), f32[8,64,128]{2,1,0:T(8,128)}) %all-reduce.18.cloned.1.call-update) | async-done | bytes 262160 | tf_op jit(solution)/shard_map/psum | solution.py:38
  436.3 1.3 fusion.26
  437.6 0.6 dynamic-slice_select_fusion.2
  438.4 0.1 copy.35
  438.5 0.1 copy.22
  438.6 63.0 %all-reduce.20.cloned.1.call-done = f32[2,64,128]{2,1,0:T(8,128)} async-done(((f32[2,64,128]{2,1,0:T(8,128)}), f32[2,64,128]{2,1,0:T(8,128)}) %all-reduce.20.cloned.1.call-update) | async-done | bytes 65552 | tf_op jit(solution)/shard_map/psum | solution.py:9
  501.6 0.9 constant_dynamic-update-slice_fusion.1
  502.5 2.5 fusion.6
  505.1 143.3 %all-reduce.22.cloned.1.call-done = f32[8,64,128]{2,1,0:T(8,128)} async-done(((f32[8,64,128]{2,1,0:T(8,128)}), f32[8,64,128]{2,1,0:T(8,128)}) %all-reduce.22.cloned.1.call-update) | async-done | bytes 262160 | tf_op jit(solution)/shard_map/psum | solution.py:38
  648.4 1.3 fusion.24
  649.7 0.6 dynamic-slice_select_fusion.1
  650.5 0.1 copy.36
  650.6 0.1 copy.24
  650.7 63.2 %all-reduce.24.cloned.1.call-done = f32[2,64,128]{2,1,0:T(8,128)} async-done(((f32[2,64,128]{2,1,0:T(8,128)}), f32[2,64,128]{2,1,0:T(8,128)}) %all-reduce.24.cloned.1.call-update) | async-done | bytes 65552 | tf_op jit(solution)/shard_map/psum | solution.py:9
  713.9 0.9 constant_dynamic-update-slice_fusion
  714.7 2.8 fusion.3
  717.6 0.1 copy.37
  717.7 0.1 copy.26
  717.8 0.6 bitcast_dynamic-update-slice_fusion.4
  718.5 142.5 %all-reduce.26.cloned.1.call-done = f32[8,64,128]{2,1,0:T(8,128)} async-done(((f32[8,64,128]{2,1,0:T(8,128)}), f32[8,64,128]{2,1,0:T(8,128)}) %all-reduce.26.cloned.1.call-update) | async-done | bytes 262160 | tf_op jit(solution)/shard_map/psum | solution.py:38
  860.9 1.3 fusion.22
  862.2 0.6 dynamic-slice_select_fusion
  862.9 0.6 bitcast_dynamic-update-slice_fusion.3
  863.6 62.8 %all-reduce.28.cloned.1.call-done = f32[2,64,128]{2,1,0:T(8,128)} async-done(((f32[2,64,128]{2,1,0:T(8,128)}), f32[2,64,128]{2,1,0:T(8,128)}) %all-reduce.28.cloned.1.call-update) | async-done | bytes 65552 | tf_op jit(solution)/shard_map/psum | solution.py:9
  926.4 0.9 bitcast_dynamic-update-slice_fusion.5
  927.3 3.0 fusion
  930.4 0.6 bitcast_dynamic-update-slice_fusion.2
  931.0 0.6 bitcast_dynamic-update-slice_fusion.1
  931.6 142.1 %all-reduce.30.cloned.1.call-done = f32[8,64,128]{2,1,0:T(8,128)} async-done(((f32[8,64,128]{2,1,0:T(8,128)}), f32[8,64,128]{2,1,0:T(8,128)}) %all-reduce.30.cloned.1.call-update) | async-done | bytes 262160 | tf_op jit(solution)/shard_map/psum | solution.py:38
  1073.7 1.3 fusion.20
  1075.0 0.6 select_bitcast_fusion
  1075.7 0.6 bitcast_dynamic-update-slice_fusion
  1076.3 62.9 %all-reduce.32.cloned.1.call-done = f32[1,2,64,128]{3,2,1,0:T(8,128)} async-done(((f32[1,2,64,128]{3,2,1,0:T(8,128)}), f32[1,2,64,128]{3,2,1,0:T(8,128)}) %all-reduce.32.cloned.1.call-update) | async-done | bytes 65552 | tf_op jit(solution)/shard_map/psum | solution.py:9
  1139.2 1.5 constant_dynamic-update-slice_fusion.4
  (48 shorter events, 1.0 us)
Async XLA Ops:
  6.5 217.7 %copy-start = (bf16[6,8,128,128]{3,2,1,0:T(8,128)(2,1)S(1)}, bf16[6,8,128,128]{3,2,1,0:T(8,128)(2,1)}, u32[]{:S(2)}) copy-start(bf16[6,8,128,128]{3,2,1,0:T(8,128)(2,1)} %param.7) | copy-start | bytes 4718596
  6.5 73.1 %copy-start.7 = (s32[15,8,2]{0,2,1:T(2,128)S(1)}, s32[15,8,2]{0,2,1:T(2,128)}, u32[]{:S(2)}) copy-start(s32[15,8,2]{0,2,1:T(2,128)} %param.6) | copy-start | bytes 2884
  6.5 71.0 %all-reduce.12.cloned.1.call-start = ((), (), s32[]{:S(2)}) async-start(), calls=%async_computation | async-start | bytes 131072 | tf_op jit(solution)/shard_map/psum | solution.py:9
  9.5 214.8 %all-reduce.14.cloned.1.call-start = ((), (), s32[]{:S(2)}) async-start(), calls=%async_computation.1 | async-start | bytes 524288 | tf_op jit(solution)/shard_map/psum | solution.py:38
  77.6 148.8 %copy-start.2 = (f32[2,64,128]{2,1,0:T(8,128)S(1)}, f32[2,64,128]{2,1,0:T(8,128)}, u32[]{:S(2)}) copy-start(f32[2,64,128]{2,1,0:T(8,128)} %all-reduce.12.cloned.1.call-done) | copy-start | bytes 196612
  79.6 210.1 %all-reduce.16.cloned.1.call-start = ((), (), s32[]{:S(2)}) async-start(), calls=%async_computation.2 | async-start | bytes 131072 | tf_op jit(solution)/shard_map/psum | solution.py:9
  80.0 356.4 %copy-start.1 = (f32[6,8,64,128]{3,2,1,0:T(8,128)S(1)}, f32[6,8,64,128]{3,2,1,0:T(8,128)}, u32[]{:S(2)}) copy-start(f32[6,8,64,128]{3,2,1,0:T(8,128)} %param.4) | copy-start | bytes 4718596
  226.3 210.0 %all-reduce.18.cloned.1.call-start = ((), (), s32[]{:S(2)}) async-start(), calls=%async_computation.3 | async-start | bytes 524288 | tf_op jit(solution)/shard_map/psum | solution.py:38
  292.9 208.8 %all-reduce.20.cloned.1.call-start = ((), (), s32[]{:S(2)}) async-start(), calls=%async_computation.4 | async-start | bytes 131072 | tf_op jit(solution)/shard_map/psum | solution.py:9
  438.3 210.1 %all-reduce.22.cloned.1.call-start = ((), (), s32[]{:S(2)}) async-start(), calls=%async_computation.5 | async-start | bytes 524288 | tf_op jit(solution)/shard_map/psum | solution.py:38
  505.0 208.8 %all-reduce.24.cloned.1.call-start = ((), (), s32[]{:S(2)}) async-start(), calls=%async_computation.6 | async-start | bytes 131072 | tf_op jit(solution)/shard_map/psum | solution.py:9
  650.4 210.6 %all-reduce.26.cloned.1.call-start = ((), (), s32[]{:S(2)}) async-start(), calls=%async_computation.7 | async-start | bytes 524288 | tf_op jit(solution)/shard_map/psum | solution.py:38
  717.5 145.5 %copy-start.3 = (f32[2,64,128]{2,1,0:T(8,128)S(1)}, f32[2,64,128]{2,1,0:T(8,128)}, u32[]{:S(2)}) copy-start(f32[2,64,128]{2,1,0:T(8,128)} %all-reduce.16.cloned.1.call-done) | copy-start | bytes 196612
  717.5 208.9 %all-reduce.28.cloned.1.call-start = ((), (), s32[]{:S(2)}) async-start(), calls=%async_computation.8 | async-start | bytes 131072 | tf_op jit(solution)/shard_map/psum | solution.py:9
  862.9 210.8 %all-reduce.30.cloned.1.call-start = ((), (), s32[]{:S(2)}) async-start(), calls=%async_computation.9 | async-start | bytes 524288 | tf_op jit(solution)/shard_map/psum | solution.py:38
  927.3 3.1 copy-start.4
  927.3 3.8 copy-start.5
  930.3 145.4 %copy-start.6 = (f32[2,64,128]{2,1,0:T(8,128)S(1)}, f32[2,64,128]{2,1,0:T(8,128)}, u32[]{:S(2)}) copy-start(f32[2,64,128]{2,1,0:T(8,128)} %all-reduce.28.cloned.1.call-done) | copy-start | bytes 196612
  930.3 208.9 %all-reduce.32.cloned.1.call-start = ((), (), s32[]{:S(2)}) async-start(), calls=%async_computation.10 | async-start | bytes 131072 | tf_op jit(solution)/shard_map/psum | solution.py:9
Sparse Core Ops, SparseCore 0:
  9.6 67.8 all-reduce.11
  81.0 143.2 all-reduce.13
  226.6 63.0 all-reduce.15
  293.0 143.2 all-reduce.17
  438.5 63.0 all-reduce.19
  505.1 143.2 all-reduce.21
  650.7 63.0 all-reduce.23
  717.6 143.2 all-reduce.25
  863.3 63.0 all-reduce.27
  930.4 143.2 all-reduce.29
  1076.0 63.0 all-reduce.31
where the time goes:
time: 1150 us
  waiting for transfers between devices  1100 us (96%)
  matrix products  19.9 us (2%)
  between operations  13.4 us (1%)
    psum x5, waiting for transfers between devices, body(): totals = lax.psum(partial_value, 'col')  716 us
    psum x6, waiting for transfers between devices, broadcast(): return lax.psum(jnp.where(mine, shard, jnp.zeros_like(shard)), axis)  382 us
  transfers between devices with their start and end apart: 11, of which 11 were waited for; matrix products, arithmetic and copies ran while one was open for 0% of the time, Pallas kernels for 0%

commit v1 on v0

--- a/solution.py
+++ b/solution.py
@@ -6,7 +6,7 @@
 
 def broadcast(shard, axis, root):
     mine = lax.axis_index(axis) == root
-    return lax.psum(jnp.where(mine, shard, jnp.zeros_like(shard)), axis)
+    return jnp.sum(lax.all_gather(jnp.where(mine, shard, jnp.zeros_like(shard)), axis), axis=0)
 
 
 def solve_rows(residual, inverse):

time: 1150 us -> 835 us (0.73)
  waiting for transfers between devices: 1100 us -> 714 us
  blocking collectives: 0 us -> 80.9 us
    psum x6 -> x0, waiting for transfers between devices: 382 us -> none  [broadcast(): return lax.psum(jnp.where(mine, shard, jnp.zeros_like(shard)), axis)]
    all_gather x0 -> x6, blocking collectives: none -> 80.9 us  [broadcast(): lax.all_gather(jnp.where(mine, shard, jnp.zeros_like(shard)), axis)]
  transfers between devices with their start and end apart: 11 -> 5, of which waited for: 11 -> 5; matrix products, arithmetic and copies ran while one was open for 0% -> 0% of each run, Pallas kernels for 0% -> 0%
where the time goes in v1:
time: 835 us; the launch traced here: 832 us
  waiting for transfers between devices  714 us (86%)
  blocking collectives  80.9 us (10%)
  matrix products  19.5 us (2%)
  between operations  13.3 us (2%)
    psum x5, waiting for transfers between devices, body(): totals = lax.psum(partial_value, 'col')  714 us
    all_gather x6, blocking collectives, broadcast(): lax.all_gather(jnp.where(mine, shard, jnp.zeros_like(shard)), axis)  80.9 us
  transfers between devices with their start and end apart: 5, of which 5 were waited for; matrix products, arithmetic and copies ran while one was open for 0% of the time, Pallas kernels for 0%

profile of v1, /device:TPU:2, one launch (start us, length us, event | category | flops | bytes accessed | tf_op | source)
XLA Modules:
  0.0 831.8 jit_solution(8829691211701518336)
XLA Ops:
  6.5 1.0 slice.66
  7.5 1.1 slice.67
  8.6 0.2 convolution_select_fusion
  8.8 13.6 %all-gather = f32[16,64,128]{2,1,0:T(8,128)S(1)} all-gather(f32[2,64,128]{2,1,0:T(8,128)S(1)} %convolution_select_fusion), channel_id=2, replica_groups=mesh['col'=32,'row'=8] {'row'}, dimensions={0}, use_global_device_ids=true | all-gather | bytes 589824 | tf_op jit(solution)/shard_map/all_gather | solution.py:9
  22.5 0.1 copy.38
  22.6 2.0 fusion.12
  24.6 0.0 all-reduce.6.cloned.1.call-update
  24.6 0.0 all-reduce.8.cloned.1.call-start
  24.6 0.1 slice.73
  24.7 0.1 copy.40
  24.8 0.1 copy.26
  24.9 146.4 %all-reduce.6.cloned.1.call-done = f32[8,64,128]{2,1,0:T(8,128)} async-done(((f32[8,64,128]{2,1,0:T(8,128)}), f32[8,64,128]{2,1,0:T(8,128)}) %all-reduce.6.cloned.1.call-update) | async-done | bytes 262160 | tf_op jit(solution)/shard_map/psum | solution.py:38
  171.3 1.4 fusion.28
  172.7 13.4 %all-gather.1 = f32[16,64,128]{2,1,0:T(8,128)S(1)} all-gather(f32[2,64,128]{2,1,0:T(8,128)S(1)} %dynamic-slice_select_fusion.4), channel_id=3, replica_groups=mesh['col'=32,'row'=8] {'row'}, dimensions={0}, use_global_device_ids=true | all-gather | bytes 589824 | tf_op jit(solution)/shard_map/all_gather | solution.py:9
  186.2 2.2 fusion.10
  188.5 0.0 all-reduce.8.cloned.1.call-update
  188.5 0.0 all-reduce.10.cloned.1.call-start
  188.5 0.1 slice.77
  188.6 0.1 copy.41
  188.7 0.1 copy.28
  188.8 141.7 %all-reduce.8.cloned.1.call-done = f32[8,64,128]{2,1,0:T(8,128)} async-done(((f32[8,64,128]{2,1,0:T(8,128)}), f32[8,64,128]{2,1,0:T(8,128)}) %all-reduce.8.cloned.1.call-update) | async-done | bytes 262160 | tf_op jit(solution)/shard_map/psum | solution.py:38
  330.5 1.4 fusion.26
  331.9 13.4 %all-gather.2 = f32[16,64,128]{2,1,0:T(8,128)S(1)} all-gather(f32[2,64,128]{2,1,0:T(8,128)S(1)} %dynamic-slice_select_fusion.3), channel_id=4, replica_groups=mesh['col'=32,'row'=8] {'row'}, dimensions={0}, use_global_device_ids=true | all-gather | bytes 589824 | tf_op jit(solution)/shard_map/all_gather | solution.py:9
  345.4 2.5 fusion.6
  347.9 0.0 all-reduce.10.cloned.1.call-update
  348.0 0.0 all-reduce.12.cloned.1.call-start
  348.0 0.1 slice.81
  348.1 0.1 slice.85
  348.2 0.1 copy.42
  348.2 0.1 copy.30
  348.4 0.1 copy.43
  348.5 0.1 copy.32
  348.6 141.5 %all-reduce.10.cloned.1.call-done = f32[8,64,128]{2,1,0:T(8,128)} async-done(((f32[8,64,128]{2,1,0:T(8,128)}), f32[8,64,128]{2,1,0:T(8,128)}) %all-reduce.10.cloned.1.call-update) | async-done | bytes 262160 | tf_op jit(solution)/shard_map/psum | solution.py:38
  490.0 1.4 fusion.24
  491.4 13.4 %all-gather.3 = f32[16,64,128]{2,1,0:T(8,128)S(1)} all-gather(f32[2,64,128]{2,1,0:T(8,128)S(1)} %dynamic-slice_select_fusion.2), channel_id=5, replica_groups=mesh['col'=32,'row'=8] {'row'}, dimensions={0}, use_global_device_ids=true | all-gather | bytes 589824 | tf_op jit(solution)/shard_map/all_gather | solution.py:9
  504.9 2.8 fusion.3
  507.7 0.0 all-reduce.12.cloned.1.call-update
  507.7 0.0 all-reduce.14.cloned.1.call-start
  507.8 142.0 %all-reduce.12.cloned.1.call-done = f32[8,64,128]{2,1,0:T(8,128)} async-done(((f32[8,64,128]{2,1,0:T(8,128)}), f32[8,64,128]{2,1,0:T(8,128)}) %all-reduce.12.cloned.1.call-update) | async-done | bytes 262160 | tf_op jit(solution)/shard_map/psum | solution.py:38
  649.8 1.4 fusion.22
  651.2 13.4 %all-gather.4 = f32[16,64,128]{2,1,0:T(8,128)S(1)} all-gather(f32[2,64,128]{2,1,0:T(8,128)S(1)} %dynamic-slice_select_fusion.1), channel_id=6, replica_groups=mesh['col'=32,'row'=8] {'row'}, dimensions={0}, use_global_device_ids=true | all-gather | bytes 589824 | tf_op jit(solution)/shard_map/all_gather | solution.py:9
  664.7 3.0 fusion
  667.7 0.0 all-reduce.14.cloned.1.call-update
  667.7 0.0 copy-start.2
  667.7 142.0 %all-reduce.14.cloned.1.call-done = f32[8,64,128]{2,1,0:T(8,128)} async-done(((f32[8,64,128]{2,1,0:T(8,128)}), f32[8,64,128]{2,1,0:T(8,128)}) %all-reduce.14.cloned.1.call-update) | async-done | bytes 262160 | tf_op jit(solution)/shard_map/psum | solution.py:38
  809.8 1.4 fusion.20
  811.2 13.4 %all-gather.5 = f32[16,64,128]{2,1,0:T(8,128)S(1)} all-gather(f32[2,64,128]{2,1,0:T(8,128)S(1)} %dynamic-slice_select_fusion), channel_id=7, replica_groups=mesh['col'=32,'row'=8] {'row'}, dimensions={0}, use_global_device_ids=true | all-gather | bytes 589824 | tf_op jit(solution)/shard_map/all_gather | solution.py:9
  824.6 0.6 bitcast_dynamic-update-slice_fusion
  (32 shorter events, 0.4 us)
Async XLA Ops:
  6.5 15.9 %copy-start.1 = (s32[15,8,2]{0,2,1:T(2,128)S(1)}, s32[15,8,2]{0,2,1:T(2,128)}, u32[]{:S(2)}) copy-start(s32[15,8,2]{0,2,1:T(2,128)} %param.6) | copy-start | bytes 2884
  6.5 164.8 %all-reduce.6.cloned.1.call-start = ((), (), s32[]{:S(2)}) async-start(), calls=%async_computation | async-start | bytes 524288 | tf_op jit(solution)/shard_map/psum | solution.py:38
  7.5 163.8 %copy-start = (bf16[6,8,128,128]{3,2,1,0:T(8,128)(2,1)S(1)}, bf16[6,8,128,128]{3,2,1,0:T(8,128)(2,1)}, u32[]{:S(2)}) copy-start(bf16[6,8,128,128]{3,2,1,0:T(8,128)(2,1)} %param.7) | copy-start | bytes 4718596
  24.6 305.9 %all-reduce.8.cloned.1.call-start = ((), (), s32[]{:S(2)}) async-start(), calls=%async_computation.1 | async-start | bytes 524288 | tf_op jit(solution)/shard_map/psum | solution.py:38
  188.5 301.5 %all-reduce.10.cloned.1.call-start = ((), (), s32[]{:S(2)}) async-start(), calls=%async_computation.2 | async-start | bytes 524288 | tf_op jit(solution)/shard_map/psum | solution.py:38
  348.0 301.8 %all-reduce.12.cloned.1.call-start = ((), (), s32[]{:S(2)}) async-start(), calls=%async_computation.3 | async-start | bytes 524288 | tf_op jit(solution)/shard_map/psum | solution.py:38
  507.7 302.1 %all-reduce.14.cloned.1.call-start = ((), (), s32[]{:S(2)}) async-start(), calls=%async_computation.4 | async-start | bytes 524288 | tf_op jit(solution)/shard_map/psum | solution.py:38
  667.7 156.9 %copy-start.2 = (f32[6,2,64,128]{3,2,1,0:T(8,128)}, f32[6,2,64,128]{3,2,1,0:T(8,128)S(1)}, u32[]{:S(2)}) copy-start(f32[6,2,64,128]{3,2,1,0:T(8,128)S(1)} %bitcast_dynamic-update-slice_fusion.1) | copy-start | bytes 1179652
Sparse Core Ops, SparseCore 0:
  24.7 146.5 all-reduce.5
  188.6 141.8 all-reduce.7
  348.1 141.9 all-reduce.9
  507.8 141.9 all-reduce.11
  667.8 141.9 all-reduce.13
